TPU v7x, 128 devices: a whole 4x4x4 slice. The times are simulated.
128 devices in a mesh: img: 8 (over y, core), fsdp: 16 (over x, z).
Axes of the slice: x: 4, y: 4, z: 4, core: 2. Of those that a mesh axis runs over, the one named last changes fastest.
Arguments:
- text_states: bfloat16 [4096, 8192], P('img', 'fsdp'), may hold values from -100 to 100, as said below
- text_gain: float32 [8192], P('fsdp'), may hold values from 0.1 to 1.9
- gate_scale: float32 [8192], P('fsdp'), may hold values from 0.3 to 1.5
- live_counts: int32 [8], P('img'), may hold values from 1 to 512, 3072 in all
- token_slot: int32 [8, 512], P('img'), may hold values from 0 to 7, never falling along the last dimension, each value on 1 to 256 neighbouring positions
- wanted_images: int32 [8, 8], replicated, may hold values from 0 to 31, as said below
- patches: bfloat16 [32, 256, 1280], P('img', None, 'fsdp'), may hold values from -100 to 100, as said below
- latent_init: bfloat16 [64, 1280], replicated, may hold values from -100 to 100, as said below
- context_gain: float32 [1280], replicated, may hold values from 0.1 to 1.9
- latent_gain: float32 [1280], replicated, may hold values from 0.1 to 1.9
- res_query: bfloat16 [1280, 1536], P(None, 'fsdp'), may hold values from -0.15625 to 0.15625
- res_key: bfloat16 [1280, 1536], P(None, 'fsdp'), may hold values from -0.15625 to 0.15625
- res_value: bfloat16 [1280, 1536], P(None, 'fsdp'), may hold values from -0.15625 to 0.15625
- res_out: bfloat16 [1536, 1280], P('fsdp'), may hold values from -0.21875 to 0.21875
- final_gain: float32 [1280], P('fsdp'), may hold values from 0.1 to 1.9
- cross_query: bfloat16 [8192, 8192], P('fsdp'), may hold values from -0.09375 to 0.09375
- cross_key: bfloat16 [1280, 8192], P('fsdp'), may hold values from -0.25 to 0.25
- cross_value: bfloat16 [1280, 8192], P('fsdp'), may hold values from -0.25 to 0.25
- cross_out: bfloat16 [8192, 8192], P('fsdp'), may hold values from -0.09375 to 0.09375
Outputs:
- layer_output: float32 [4096, 8192], P('img', 'fsdp')
Inputs may be any that keep to these rules, and one draw needn't show every extreme that they name: `wanted_images`: image i is held by owner i // 4 along img. A row lists 8 distinct images; every owner that appears in a row has exactly 2 of its images there. `token_slot`: along a shard's tokens the slot never falls, and every slot of the shard is used. Tokens of shard s at positions live_counts[s] and beyond are padding. `text_states`: real values. `patches`: real values. `latent_init`: real values.
All inputs are finite; a program needn't handle non-finite values.
Results may differ from a plain program's by a relative error of at most 0.0075.
Values may be sent and summed in bfloat16 or wider, within the bound.
No kernel may reach another device: no remote copies, remote signals or barrier semaphores. Data moves between devices by JAX's collectives and lax.ppermute only.
A program may use at most 128 MiB of HBM per device.

v0:
```python
import jax
import jax.numpy as jnp
from jax import lax
from jax.sharding import PartitionSpec as P

D = 8192
HEAD = 128
RHD = 96
PAIR = 2
eps_norm = 1e-05
eps_rms = 1e-06


def layer_norm(values, gain_vec):
    values = values.astype(jnp.float32)
    row_mean = jnp.mean(values, -1, keepdims=True)
    spread = jnp.mean(values * values, -1, keepdims=True) - row_mean * row_mean
    return (values - row_mean) * lax.rsqrt(spread + eps_norm) * gain_vec


def route_tables(wanted_images, per_owner, pair_slots):
    owners = wanted_images // per_owner
    slot_total = wanted_images.shape[1]
    positions = jnp.arange(slot_total, dtype=jnp.int32)
    before = (owners[:, :, None] == owners[:, None, :]) & (
        positions[None, None, :] < positions[None, :, None]
    )
    slot_rank = jnp.sum(before.astype(jnp.int32), axis=2)
    rank_hot = (
        slot_rank[:, :, None] == jnp.arange(pair_slots, dtype=jnp.int32)[None, None, :]
    ).astype(jnp.float32)
    return (owners, rank_hot)


def pack_rows(row_data, wanted_images, my_shard, per_owner, pair_slots):
    owners, rank_hot = route_tables(wanted_images, per_owner, pair_slots)
    is_mine = (owners == my_shard).astype(jnp.float32)
    local_hot = (
        (wanted_images % per_owner)[:, :, None]
        == jnp.arange(per_owner, dtype=jnp.int32)[None, None, :]
    ).astype(jnp.float32)
    picker = jnp.einsum("scp,sci->spi", rank_hot * is_mine[:, :, None], local_hot).astype(
        jnp.bfloat16
    )
    return jnp.einsum("spi,if->spf", picker, row_data, preferred_element_type=jnp.float32).astype(
        jnp.bfloat16
    )


def unpack_rows(received, wanted_images, my_shard, per_owner, pair_slots):
    owners, rank_hot = route_tables(wanted_images, per_owner, pair_slots)
    owner_row = lax.dynamic_slice_in_dim(owners, my_shard, 1, 0)[0]
    rank_row = lax.dynamic_slice_in_dim(rank_hot, my_shard, 1, 0)[0]
    source_hot = (
        owner_row[:, None] == jnp.arange(received.shape[0], dtype=jnp.int32)[None, :]
    ).astype(jnp.float32)
    taker = (source_hot[:, :, None] * rank_row[:, None, :]).astype(jnp.bfloat16)
    return jnp.einsum("cop,opf->cf", taker, received, preferred_element_type=jnp.float32).astype(
        jnp.bfloat16
    )


def keyval_partial(flat_rows, cross_key, cross_value, head_cols, row_count):
    contract_first = (((0,), (1,)), ((), ()))
    block_count = row_count // (2 * head_cols)
    key_cols = lax.dot_general(
        cross_key, flat_rows, contract_first, preferred_element_type=jnp.float32
    )
    value_cols = lax.dot_general(
        cross_value, flat_rows, contract_first, preferred_element_type=jnp.float32
    )
    key_cols = key_cols.reshape(block_count, head_cols, flat_rows.shape[0])
    value_cols = value_cols.reshape(block_count, head_cols, flat_rows.shape[0])
    return jnp.concatenate([key_cols, value_cols], 1).reshape(row_count, flat_rows.shape[0])


def local(
    text_states,
    text_gain,
    gate_scale,
    live_counts,
    token_slot,
    wanted_images,
    patches,
    latent_init,
    context_gain,
    latent_gain,
    res_query,
    res_key,
    res_value,
    res_out,
    final_gain,
    cross_query,
    cross_key,
    cross_value,
    cross_out,
):
    my_feature = lax.axis_index("fsdp")
    my_shard = lax.axis_index("img")
    image_count = patches.shape[0]
    patch_count = patches.shape[1]
    feat_vis = patches.shape[2]
    latent_count = latent_init.shape[0]
    vis_width = latent_init.shape[1]
    res_cols = res_query.shape[1]
    res_heads = res_cols // RHD
    head_cols = cross_out.shape[0]
    token_count = text_states.shape[0]
    slot_count = wanted_images.shape[1]
    cross_heads = head_cols // HEAD
    contract_first = (((0,), (1,)), ((), ()))
    full_patches = lax.all_gather(patches, "fsdp", axis=2, tiled=True)
    context = layer_norm(full_patches, context_gain).astype(jnp.bfloat16)
    latent_normed = layer_norm(latent_init, latent_gain).astype(jnp.bfloat16)
    res_q_rows = jnp.dot(latent_normed, res_query, preferred_element_type=jnp.float32).astype(
        jnp.bfloat16
    )
    res_q_rows = res_q_rows.reshape(latent_count, res_heads, RHD)
    ctx_keys = jnp.einsum(
        "npv,vk->npk", context, res_key, preferred_element_type=jnp.float32
    ).astype(jnp.bfloat16)
    ctx_values = jnp.einsum(
        "npv,vk->npk", context, res_value, preferred_element_type=jnp.float32
    ).astype(jnp.bfloat16)
    lat_keys = jnp.dot(latent_normed, res_key, preferred_element_type=jnp.float32).astype(
        jnp.bfloat16
    )
    lat_values = jnp.dot(latent_normed, res_value, preferred_element_type=jnp.float32).astype(
        jnp.bfloat16
    )
    joined_shape = (image_count, latent_count, res_cols)
    key_rows = jnp.concatenate([ctx_keys, jnp.broadcast_to(lat_keys[None], joined_shape)], 1)
    value_rows = jnp.concatenate([ctx_values, jnp.broadcast_to(lat_values[None], joined_shape)], 1)
    key_rows = key_rows.reshape(image_count, patch_count + latent_count, res_heads, RHD)
    value_rows = value_rows.reshape(image_count, patch_count + latent_count, res_heads, RHD)
    res_scores = jnp.einsum(
        "rhe,nkhe->nhrk", res_q_rows, key_rows, preferred_element_type=jnp.float32
    ) * RHD ** (-0.5)
    res_weights = jnp.exp(res_scores)
    res_weights = (res_weights / jnp.sum(res_weights, -1, keepdims=True)).astype(jnp.bfloat16)
    res_mixed = jnp.einsum(
        "nhrk,nkhe->nrhe", res_weights, value_rows, preferred_element_type=jnp.float32
    )
    res_mixed = res_mixed.astype(jnp.bfloat16).reshape(image_count * latent_count, res_cols)
    columns = res_out
    mixed_sum = lax.psum_scatter(
        lax.dot_general(
            columns, res_mixed, contract_first, preferred_element_type=jnp.float32
        ).astype(jnp.bfloat16),
        "fsdp",
        scatter_dimension=0,
        tiled=True,
    ).astype(jnp.float32)
    init_cols = lax.dynamic_slice_in_dim(latent_init, my_feature * feat_vis, feat_vis, 1).astype(
        jnp.float32
    )
    latents = init_cols[None] + jnp.transpose(mixed_sum).reshape(
        image_count, latent_count, feat_vis
    )
    sum_first, sum_second = lax.psum((jnp.sum(latents, -1), jnp.sum(latents * latents, -1)), "fsdp")
    row_mean = sum_first / vis_width
    spread = sum_second / vis_width - row_mean * row_mean
    resampled = (
        (latents - row_mean[..., None]) * lax.rsqrt(spread + eps_norm)[..., None] * final_gain
    ).astype(jnp.bfloat16)
    text_f = text_states.astype(jnp.float32)
    squares = lax.psum(jnp.sum(text_f * text_f, -1), "fsdp")
    normed = (text_f * lax.rsqrt(squares / D + eps_rms)[:, None] * text_gain).astype(jnp.bfloat16)
    columns = cross_query
    query_cols = lax.psum_scatter(
        lax.dot_general(columns, normed, contract_first, preferred_element_type=jnp.float32).astype(
            jnp.bfloat16
        ),
        "fsdp",
        scatter_dimension=0,
        tiled=True,
    )
    per_image = resampled.reshape(image_count, latent_count * feat_vis)
    outgoing = pack_rows(per_image, wanted_images, my_shard, image_count, PAIR)
    incoming = lax.all_to_all(outgoing, "img", split_axis=0, concat_axis=0, tiled=True)
    slot_latents = unpack_rows(incoming, wanted_images, my_shard, image_count, PAIR).reshape(
        slot_count * latent_count, feat_vis
    )
    slot_kv = lax.psum_scatter(
        keyval_partial(
            slot_latents, cross_key, cross_value, head_cols, 2 * head_cols * lax.axis_size("fsdp")
        ).astype(jnp.bfloat16),
        "fsdp",
        scatter_dimension=0,
        tiled=True,
    )
    kv_slots = jnp.transpose(slot_kv.reshape(2 * head_cols, slot_count, latent_count), (1, 0, 2))
    query_heads = query_cols.reshape(cross_heads, HEAD, token_count)
    slot_keys = kv_slots[:, :head_cols].reshape(slot_count, cross_heads, HEAD, latent_count)
    slot_values = kv_slots[:, head_cols:].reshape(slot_count, cross_heads, HEAD, latent_count)
    scores = jnp.einsum(
        "het,cher->htcr", query_heads, slot_keys, preferred_element_type=jnp.float32
    ) * HEAD ** (-0.5)
    slot_hot = (token_slot[0][:, None] == jnp.arange(slot_count, dtype=jnp.int32)[None, :]).astype(
        jnp.float32
    )
    weights = jnp.exp(scores) * slot_hot[None, :, :, None]
    weights = (weights / jnp.sum(weights, axis=(2, 3), keepdims=True)).astype(jnp.bfloat16)
    attended = jnp.einsum(
        "htcr,cher->het", weights, slot_values, preferred_element_type=jnp.float32
    )
    attended = attended.astype(jnp.bfloat16).reshape(head_cols, token_count)
    columns = cross_out
    projected_cols = lax.psum_scatter(
        lax.dot_general(
            columns, attended, (((0,), (0,)), ((), ())), preferred_element_type=jnp.float32
        ).astype(jnp.bfloat16),
        "fsdp",
        scatter_dimension=0,
        tiled=True,
    ).astype(jnp.float32)
    projected = jnp.transpose(projected_cols)
    positions = jnp.arange(token_count, dtype=jnp.int32)
    live_mask = (positions < live_counts[0]).astype(jnp.float32)[:, None]
    return text_f + jnp.tanh(gate_scale) * projected * live_mask


def solution(mesh):
    placed = (
        P("img", "fsdp"),
        P("fsdp"),
        P("fsdp"),
        P("img"),
        P("img", None),
        P(),
        P("img", None, "fsdp"),
        P(),
        P(),
        P(),
        P(None, "fsdp"),
        P(None, "fsdp"),
        P(None, "fsdp"),
        P("fsdp", None),
        P("fsdp"),
        P("fsdp", None),
        P("fsdp", None),
        P("fsdp", None),
        P("fsdp", None),
    )
    return jax.shard_map(
        local, mesh=mesh, in_specs=placed, out_specs=P("img", "fsdp"), check_vma=False
    )
```

profile of v0, /device:TPU:0, one launch (start us, length us, event | category | flops | bytes accessed | tf_op | source)
XLA Modules:
  0.0 494.0 jit_solution(16812852713913608499)
XLA Ops:
  8.4 1.3 convolution_convert_fusion.10
  9.8 1.3 convolution_convert_fusion.11
  11.3 46.9 %all-gather.2.cloned.1.call-done = bf16[4,256,1280]{1,2,0:T(8,128)(2,1)} async-done(((bf16[4,256,80]{1,2,0:T(8,128)(2,1)}), bf16[4,256,1280]{1,2,0:T(8,128)(2,1)}) %all-gather.2.cloned.1.call-update) | async-done | bytes 2621456 | tf_op jit(solution)/shard_map/all_gather | solution.py:112
  58.2 2.4 convert_reduce_fusion
  60.6 2.8 convolution_convert_fusion.6
  64.2 2.8 convolution_convert_fusion.7
  69.1 72.8 %reduce-scatter.13.cloned.1.call-done = bf16[80,256]{1,0:T(8,128)(2,1)} async-done(((bf16[1280,256]{1,0:T(8,128)(2,1)}), bf16[80,256]{1,0:T(8,128)(2,1)}) %reduce-scatter.13.cloned.1.call-update) | async-done | bytes 40976
  143.1 38.6 %all-reduce = (f32[512]{0:T(512)S(1)}, f32[4,64]{1,0:T(4,128)S(1)}, f32[4,64]{1,0:T(4,128)S(1)}) all-reduce(f32[512]{0:T(512)S(1)} %fusion.15, f32[4,64]{1,0:T(4,128)S(1)} %reduce_sum.107, f32[4,64]{1,0:T(4,128)S(1)} %reduce_sum.105), channel_id=1, replica_groups=mesh['img'=8,'fsdp'=16] {'fsdp'}, use_global_device_ids=true, to_apply=%region_13.14 | all-reduce | flops 1024 | bytes 8192 | tf_op jit(solution)/shard_map/psum | solution.py:167
  181.7 10.2 %fusion = bf16[8192,512]{0,1:T(8,128)(2,1)} fusion(bf16[512,8192]{1,0:T(8,128)(2,1)} %param.34, bf16[512,512]{1,0:T(8,128)(2,1)S(1)} %copy-done.2, f32[512]{0:T(512)S(1)} %copy-done.14, f32[512]{0:T(512)S(1)} %add_rsqrt_fusion.1), kind=kOutput, calls=%fused_computation.5 | convolution fusion | flops 4300210176 | bytes 17305600 | tf_op jit(solution)/shard_map/dot_general | solution.py:171
  194.9 4.3 all-to-all-start
  199.5 6.2 %all-to-all-done = bf16[8,2,5120]{2,1,0:T(2,128)(2,1)S(1)} async-done(((bf16[8,2,5120]{2,1,0:T(2,128)(2,1)}), bf16[8,2,5120]{2,1,0:T(2,128)(2,1)S(1)}, u32[]{:S(2)}, u32[]{:S(2)}) %all-to-all-start) | async-done | bytes 163872 | tf_op jit(solution)/shard_map/all_to_all | solution.py:180
  206.1 5.6 %convolution_convert_fusion.3 = bf16[512,8192]{1,0:T(8,128)(2,1)} fusion(bf16[512,80]{1,0:T(8,128)(2,1)S(1)} %reshape.194, bf16[80,8192]{1,0:T(8,128)(2,1)S(1)} %copy-done), kind=kOutput, calls=%fused_computation.4 | convolution fusion | flops 675282944 | bytes 9781248 | tf_op jit(solution)/shard_map/dot_general | solution.py:66
  211.7 11.6 %copy.53 = bf16[64,8,16,512]{3,2,1,0:T(8,128)(2,1)} copy(bf16[64,8,16,512]{3,1,2,0:T(8,128)(2,1)} %bitcast.115) | data formatting | bytes 16777216
  223.2 5.5 %convolution_convert_fusion.2 = bf16[512,8192]{1,0:T(8,128)(2,1)} fusion(bf16[512,80]{1,0:T(8,128)(2,1)S(1)} %reshape.194, bf16[80,8192]{1,0:T(8,128)(2,1)S(1)} %copy-done.3), kind=kOutput, calls=%fused_computation.3 | convolution fusion | flops 675282944 | bytes 9781248 | tf_op jit(solution)/shard_map/dot_general | solution.py:69
  228.8 11.4 %copy.54 = bf16[64,8,16,512]{3,2,1,0:T(8,128)(2,1)} copy(bf16[64,8,16,512]{3,1,2,0:T(8,128)(2,1)} %bitcast.114) | data formatting | bytes 16777216
  240.2 8.4 %pad_maximum_fusion = bf16[16,1024,512]{1,0,2:T(8,128)(2,1)S(1)} fusion(bf16[16,512,512]{1,0,2:T(8,128)(2,1)} %bitcast.117, bf16[16,512,512]{1,0,2:T(8,128)(2,1)} %bitcast.116), kind=kLoop, calls=%fused_computation | loop fusion | flops 33554432 | bytes 33554432 | tf_op jit(solution)/shard_map/concatenate | solution.py:74
  248.6 12.0 %copy.55 = bf16[64,8,16,1024]{3,1,2,0:T(8,128)(2,1)} copy(bf16[64,8,16,1024]{3,2,1,0:T(8,128)(2,1)S(1)} %bitcast.113) | data formatting | bytes 33554432
  261.3 13.3 %reduce-scatter.9.cloned.1.call-done = bf16[512,512]{0,1:T(8,128)(2,1)} async-done(((bf16[8192,512]{0,1:T(8,128)(2,1)}), bf16[512,512]{0,1:T(8,128)(2,1)}) %reduce-scatter.9.cloned.1.call-update) | async-done | bytes 524304 | tf_op jit(solution)/shard_map/reduce_scatter | solution.py:170
  275.8 112.3 %reduce-scatter.7.cloned.1.call-done = bf16[1024,512]{0,1:T(8,128)(2,1)} async-done(((bf16[16384,512]{0,1:T(8,128)(2,1)}), bf16[1024,512]{0,1:T(8,128)(2,1)}) %reduce-scatter.7.cloned.1.call-update) | async-done | bytes 1048592 | tf_op jit(solution)/shard_map/reduce_scatter | solution.py:184
  388.1 1.3 slice_bitcast_fusion.1
  391.6 1.5 slice-done.1
  393.1 6.9 %fusion.1 = bf16[8192,512]{0,1:T(8,128)(2,1)} fusion(bf16[512,512]{1,0:T(8,128)(2,1)S(1)} %bitcast.122, bf16[512,8192]{1,0:T(8,128)(2,1)S(1)} %bitcast.119), kind=kOutput, calls=%fused_computation.6 | convolution fusion | flops 4299161600 | bytes 17301504 | tf_op jit(solution)/shard_map/dot_general | solution.py:210
  400.8 84.4 %reduce-scatter.11.cloned.1.call-done = bf16[512,512]{0,1:T(8,128)(2,1)} async-done(((bf16[8192,512]{0,1:T(8,128)(2,1)}), bf16[512,512]{0,1:T(8,128)(2,1)}) %reduce-scatter.11.cloned.1.call-update) | async-done | bytes 524304 | tf_op jit(solution)/shard_map/reduce_scatter | solution.py:209
  485.3 2.2 convert_add_fusion
  (91 shorter events, 13.7 us)
Async XLA Ops:
  6.5 199.6 %copy-start = (bf16[80,8192]{1,0:T(8,128)(2,1)S(1)}, bf16[80,8192]{1,0:T(8,128)(2,1)}, u32[]{:S(2)}) copy-start(bf16[80,8192]{1,0:T(8,128)(2,1)} %param.35) | copy-start | bytes 3932164
  6.5 56.9 %copy-start.5 = (bf16[64,1280]{1,0:T(8,128)(2,1)S(1)}, bf16[64,1280]{1,0:T(8,128)(2,1)}, u32[]{:S(2)}) copy-start(bf16[64,1280]{1,0:T(8,128)(2,1)} %param.26) | copy-start | bytes 491524
  6.5 56.9 %copy-start.12 = (f32[1280]{0:T(1024)S(1)}, f32[1280]{0:T(1024)}, u32[]{:S(2)}) copy-start(f32[1280]{0:T(1024)} %param.28) | copy-start | bytes 15364
  6.5 56.9 %copy-start.10 = (bf16[1280,96]{0,1:T(8,128)(2,1)S(1)}, bf16[1280,96]{0,1:T(8,128)(2,1)}, u32[]{:S(2)}) copy-start(bf16[1280,96]{0,1:T(8,128)(2,1)} %param.29) | copy-start | bytes 737284
  6.5 51.6 %all-gather.2.cloned.1.call-start = ((), (), s32[]{:S(2)}) async-start(), calls=%async_computation.5 | async-start | bytes 2785280 | tf_op jit(solution)/shard_map/all_gather | solution.py:112
  7.3 134.6 %reduce-scatter.13.cloned.1.call-start = ((), (), s32[]{:S(2)}) async-start(), calls=%async_computation.9 | async-start | bytes 696320
  9.8 54.3 %copy-start.11 = (bf16[1280,96]{0,1:T(8,128)(2,1)S(1)}, bf16[1280,96]{0,1:T(8,128)(2,1)}, u32[]{:S(2)}) copy-start(bf16[1280,96]{0,1:T(8,128)(2,1)} %param.31) | copy-start | bytes 737284
  9.8 54.3 %copy-start.13 = (f32[1280]{0:T(1024)S(1)}, f32[1280]{0:T(1024)}, u32[]{:S(2)}) copy-start(f32[1280]{0:T(1024)} %param.27) | copy-start | bytes 15364
  63.4 3.9 copy-start.4
  64.1 4.8 copy-start.2
  64.1 117.5 %copy-start.14 = (f32[512]{0:T(512)S(1)}, f32[512]{0:T(512)}, u32[]{:S(2)}) copy-start(f32[512]{0:T(512)} %param.20) | copy-start | bytes 6148
  68.8 205.8 %reduce-scatter.9.cloned.1.call-start = ((), (), s32[]{:S(2)}) async-start(), calls=%async_computation.7 | async-start | bytes 8912896 | tf_op jit(solution)/shard_map/reduce_scatter | solution.py:170
  191.9 0.7 copy-start.9
  191.9 0.7 copy-start.6
  194.9 10.7 %all-to-all-start = ((bf16[8,2,5120]{2,1,0:T(2,128)(2,1)}), bf16[8,2,5120]{2,1,0:T(2,128)(2,1)S(1)}, u32[]{:S(2)}, u32[]{:S(2)}) async-start(bf16[8,2,5120]{2,1,0:T(2,128)(2,1)} %copy.39), calls=%async_computation | async-start | bytes 327680 | tf_op jit(solution)/shard_map/all_to_all | solution.py:180
  199.2 188.9 %reduce-scatter.7.cloned.1.call-start = ((), (), s32[]{:S(2)}) async-start(), calls=%async_computation.6 | async-start | bytes 17825792 | tf_op jit(solution)/shard_map/reduce_scatter | solution.py:184
  211.7 11.6 %copy-start.3 = (bf16[80,8192]{1,0:T(8,128)(2,1)S(1)}, bf16[80,8192]{1,0:T(8,128)(2,1)}, u32[]{:S(2)}) copy-start(bf16[80,8192]{1,0:T(8,128)(2,1)} %param.36) | copy-start | bytes 3932164
  260.6 0.7 copy-start.7
  260.6 224.7 %reduce-scatter.11.cloned.1.call-start = ((), (), s32[]{:S(2)}) async-start(), calls=%async_computation.8 | async-start | bytes 8912896 | tf_op jit(solution)/shard_map/reduce_scatter | solution.py:209
  389.4 2.2 slice-start
  390.3 2.8 slice-start.1
  400.0 0.8 copy-start.8
  400.0 87.5 %copy-start.1 = (bf16[80,8192]{1,0:T(8,128)(2,1)S(1)}, bf16[80,8192]{1,0:T(8,128)(2,1)}, u32[]{:S(2)}) copy-start(bf16[80,8192]{1,0:T(8,128)(2,1)} %param.35) | copy-start | bytes 3932164
Sparse Core Ops, SparseCore 0:
  9.5 48.6 all-gather.1
  68.9 72.9 reduce-scatter.12
  192.1 82.4 reduce-scatter.8
  277.8 110.2 reduce-scatter.6
  400.2 85.0 reduce-scatter.10
where the time goes:
time: 495 us; the launch traced here: 494 us
  waiting for transfers between devices  337 us (68%)
  local copies, waits for them, and re-layouts  44.7 us (9%)
  matrix products  40.3 us (8%)
  blocking collectives  38.6 us (8%)
  other arithmetic  14.9 us (3%)
  between operations  14.3 us (3%)
    reduce_scatter x1, waiting for transfers between devices, local(): lax.psum_scatter(keyval_partial(slot_latents, cross_key, cross_value, hea...  112 us
    reduce_scatter x1, waiting for transfers between devices, local(): lax.psum_scatter(lax.dot_general(columns, attended, (((0,), (0,)), ((), (...  84.4 us
    unnamed x6, waiting for transfers between devices  73.5 us
    all_gather x1, waiting for transfers between devices, local(): full_patches = lax.all_gather(patches, 'fsdp', axis=2, tiled=True)  46.9 us
    unnamed x40, local copies, waits for them, and re-layouts  41.2 us
    psum x1, blocking collectives, local(): squares = lax.psum(jnp.sum(text_f * text_f, -1), 'fsdp')  38.6 us
    reduce_scatter x1, waiting for transfers between devices, local(): lax.psum_scatter(lax.dot_general(columns, normed, contract_first, preferr...  13.3 us
    dot_general x1, matrix products, local(): lax.dot_general(columns, normed, contract_first, preferred_element_type=j...  10.2 us
  transfers between devices with their start and end apart: 6, of which 6 were waited for; matrix products, arithmetic and copies ran while one was open for 13% of the time, Pallas kernels for 0%

commit v1 on v0

--- a/solution.py
+++ b/solution.py
@@ -9,6 +9,19 @@
 PAIR = 2
 eps_norm = 1e-05
 eps_rms = 1e-06
+
+
+def collect(value, axis, dim):
+    ways = lax.axis_size(axis)
+    up = [(d, (d + 1) % ways) for d in range(ways)]
+    down = [(d, (d - 1) % ways) for d in range(ways)]
+    earlier, later = ([value], [value])
+    for _ in range(ways // 2):
+        earlier.append(lax.ppermute(earlier[-1], axis, up))
+    for _ in range((ways - 1) // 2):
+        later.append(lax.ppermute(later[-1], axis, down))
+    line = jnp.concatenate([*earlier[::-1], *later[1:]], axis=dim)
+    return jnp.roll(line, (lax.axis_index(axis) - ways // 2) * value.shape[dim], axis=dim)
 
 
 def layer_norm(values, gain_vec):
@@ -109,7 +122,7 @@
     slot_count = wanted_images.shape[1]
     cross_heads = head_cols // HEAD
     contract_first = (((0,), (1,)), ((), ()))
-    full_patches = lax.all_gather(patches, "fsdp", axis=2, tiled=True)
+    full_patches = collect(patches, "fsdp", 2)
     context = layer_norm(full_patches, context_gain).astype(jnp.bfloat16)
     latent_normed = layer_norm(latent_init, latent_gain).astype(jnp.bfloat16)
     res_q_rows = jnp.dot(latent_normed, res_query, preferred_element_type=jnp.float32).astype(

time: 495 us -> 529 us (1.069); the launches traced: 494 us -> 520 us
  starting transfers between devices: 4.66 us -> 45.2 us
  waiting for transfers between devices: 337 us -> 318 us
    all_gather x1 -> x0, waiting for transfers between devices: 46.9 us -> none  [local(): full_patches = lax.all_gather(patches, 'fsdp', axis=2, tiled=True)]
    ppermute x0 -> x15, starting transfers between devices: none -> 40.8 us  [the longest x7 38.8 us: collect(): later.append(lax.ppermute(later[-1], axis, down))]
    ppermute x0 -> x15, waiting for transfers between devices: none -> 28.4 us  [the longest x8 27.7 us: collect(): earlier.append(lax.ppermute(earlier[-1], axis, up))]
    unnamed x40 -> x75, local copies, waits for them, and re-layouts: 41.2 us -> 46.2 us
    unnamed x6 -> x5, waiting for transfers between devices: 73.5 us -> 73.3 us
  transfers between devices with their start and end apart: 6 -> 20, of which waited for: 6 -> 14; matrix products, arithmetic and copies ran while one was open for 13% -> 13% of each run, Pallas kernels for 0% -> 0%
where the time goes in v1:
time: 529 us; the launch traced here: 520 us
  waiting for transfers between devices  318 us (60%)
  local copies, waits for them, and re-layouts  49.7 us (9%)
  starting transfers between devices  45.2 us (9%)
  matrix products  39.1 us (7%)
  blocking collectives  39 us (7%)
  between operations  14.8 us (3%)
  other arithmetic  13.6 us (3%)
    reduce_scatter x1, waiting for transfers between devices, local(): lax.psum_scatter(keyval_partial(slot_latents, cross_key, cross_value, hea...  112 us
    reduce_scatter x1, waiting for transfers between devices, local(): lax.psum_scatter(lax.dot_general(columns, attended, (((0,), (0,)), ((), (...  84.6 us
    unnamed x5, waiting for transfers between devices  73.3 us
    unnamed x75, local copies, waits for them, and re-layouts  46.2 us
    psum x1, blocking collectives, local(): squares = lax.psum(jnp.sum(text_f * text_f, -1), 'fsdp')  39 us
    ppermute x7, starting transfers between devices, collect(): later.append(lax.ppermute(later[-1], axis, down))  38.8 us
    ppermute x8, waiting for transfers between devices, collect(): earlier.append(lax.ppermute(earlier[-1], axis, up))  27.7 us
    reduce_scatter x1, waiting for transfers between devices, local(): lax.psum_scatter(lax.dot_general(columns, normed, contract_first, preferr...  13.1 us
  transfers between devices with their start and end apart: 20, of which 14 were waited for; matrix products, arithmetic and copies ran while one was open for 13% of the time, Pallas kernels for 0%

profile of v1, /device:TPU:0, one launch (start us, length us, event | category | flops | bytes accessed | tf_op | source)
XLA Modules:
  0.0 519.5 jit_solution(6277490290760624686)
XLA Ops:
  8.6 8.8 %collective-permute-done = bf16[4,256,80]{1,2,0:T(8,128)(2,1)S(1)} collective-permute-done((bf16[4,256,80]{1,2,0:T(8,128)(2,1)}, bf16[4,256,80]{1,2,0:T(8,128)(2,1)S(1)}, u32[]{:S(2)}, u32[]{:S(2)}) %collective-permute-start) | collective-permute-done | bytes 163872 | tf_op jit(solution)/shard_map/ppermute | solution.py:20
  17.3 5.3 %collective-permute-start.8 = (bf16[4,256,80]{1,2,0:T(8,128)(2,1)}, bf16[4,256,80]{1,2,0:T(8,128)(2,1)S(1)}, u32[]{:S(2)}, u32[]{:S(2)}) collective-permute-start(bf16[4,256,80]{1,2,0:T(8,128)(2,1)} %param.25), channel_id=1, source_target_pairs={{0,15},{1,0},{2,1},{3,2},{4,3},{5,4},{6,5},{7,6},{8,7},{9,8},{10,9... | collective-permute-start | bytes 491528 | tf_op jit(solution)/shard_map/ppermute | solution.py:22
  22.7 3.3 collective-permute-done.1
  26.0 5.5 %collective-permute-start.9 = (bf16[4,256,80]{1,2,0:T(8,128)(2,1)S(1)}, bf16[4,256,80]{1,2,0:T(8,128)(2,1)S(1)}, u32[]{:S(2)}, u32[]{:S(2)}) collective-permute-start(bf16[4,256,80]{1,2,0:T(8,128)(2,1)S(1)} %collective-permute-done.8), channel_id=1, source_target_pairs={{0,15},{1,0},{2,1},{3,2},{4,3},{5,4},{6,5},{7,6},{8,7},{9,8},{10,9... | collective-permute-start | bytes 491528 | tf_op jit(solution)/shard_map/ppermute | solution.py:22
  34.7 5.5 %collective-permute-start.10 = (bf16[4,256,80]{1,2,0:T(8,128)(2,1)S(1)}, bf16[4,256,80]{1,2,0:T(8,128)(2,1)S(1)}, u32[]{:S(2)}, u32[]{:S(2)}) collective-permute-start(bf16[4,256,80]{1,2,0:T(8,128)(2,1)S(1)} %collective-permute-done.9), channel_id=1, source_target_pairs={{0,15},{1,0},{2,1},{3,2},{4,3},{5,4},{6,5},{7,6},{8,7},{9,8},{10,9... | collective-permute-start | bytes 491528 | tf_op jit(solution)/shard_map/ppermute | solution.py:22
  44.4 5.4 %collective-permute-start.11 = (bf16[4,256,80]{1,2,0:T(8,128)(2,1)S(1)}, bf16[4,256,80]{1,2,0:T(8,128)(2,1)S(1)}, u32[]{:S(2)}, u32[]{:S(2)}) collective-permute-start(bf16[4,256,80]{1,2,0:T(8,128)(2,1)S(1)} %collective-permute-done.10), channel_id=1, source_target_pairs={{0,15},{1,0},{2,1},{3,2},{4,3},{5,4},{6,5},{7,6},{8,7},{9,8},{10,9... | collective-permute-start | bytes 491528 | tf_op jit(solution)/shard_map/ppermute | solution.py:22
  52.6 5.8 %collective-permute-start.12 = (bf16[4,256,80]{1,2,0:T(8,128)(2,1)S(1)}, bf16[4,256,80]{1,2,0:T(8,128)(2,1)S(1)}, u32[]{:S(2)}, u32[]{:S(2)}) collective-permute-start(bf16[4,256,80]{1,2,0:T(8,128)(2,1)S(1)} %collective-permute-done.11), channel_id=1, source_target_pairs={{0,15},{1,0},{2,1},{3,2},{4,3},{5,4},{6,5},{7,6},{8,7},{9,8},{10,9... | collective-permute-start | bytes 491528 | tf_op jit(solution)/shard_map/ppermute | solution.py:22
  62.3 5.4 %collective-permute-start.13 = (bf16[4,256,80]{1,2,0:T(8,128)(2,1)S(1)}, bf16[4,256,80]{1,2,0:T(8,128)(2,1)S(1)}, u32[]{:S(2)}, u32[]{:S(2)}) collective-permute-start(bf16[4,256,80]{1,2,0:T(8,128)(2,1)S(1)} %collective-permute-done.12), channel_id=1, source_target_pairs={{0,15},{1,0},{2,1},{3,2},{4,3},{5,4},{6,5},{7,6},{8,7},{9,8},{10,9... | collective-permute-start | bytes 491528 | tf_op jit(solution)/shard_map/ppermute | solution.py:22
  72.1 5.8 %collective-permute-start.14 = (bf16[4,256,80]{1,2,0:T(8,128)(2,1)S(1)}, bf16[4,256,80]{1,2,0:T(8,128)(2,1)S(1)}, u32[]{:S(2)}, u32[]{:S(2)}) collective-permute-start(bf16[4,256,80]{1,2,0:T(8,128)(2,1)S(1)} %collective-permute-done.13), channel_id=1, source_target_pairs={{0,15},{1,0},{2,1},{3,2},{4,3},{5,4},{6,5},{7,6},{8,7},{9,8},{10,9... | collective-permute-start | bytes 491528 | tf_op jit(solution)/shard_map/ppermute | solution.py:22
  93.4 73.2 %reduce-scatter.13.cloned.1.call-done = bf16[80,256]{1,0:T(8,128)(2,1)} async-done(((bf16[1280,256]{1,0:T(8,128)(2,1)}), bf16[80,256]{1,0:T(8,128)(2,1)}) %reduce-scatter.13.cloned.1.call-update) | async-done | bytes 40976
  167.8 39.0 %all-reduce = (f32[512]{0:T(512)S(1)}, f32[4,64]{1,0:T(4,128)S(1)}, f32[4,64]{1,0:T(4,128)S(1)}) all-reduce(f32[512]{0:T(512)S(1)} %fusion.15, f32[4,64]{1,0:T(4,128)S(1)} %reduce_sum.107, f32[4,64]{1,0:T(4,128)S(1)} %reduce_sum.105), channel_id=1, replica_groups=mesh['img'=8,'fsdp'=16] {'fsdp'}, use_global_device_ids=true, to_apply=%region_13.14 | all-reduce | flops 1024 | bytes 8192 | tf_op jit(solution)/shard_map/psum | solution.py:180
  206.8 10.3 %fusion = bf16[8192,512]{0,1:T(8,128)(2,1)} fusion(bf16[512,8192]{1,0:T(8,128)(2,1)} %param.34, bf16[512,512]{1,0:T(8,128)(2,1)S(1)} %copy-done.2, f32[512]{0:T(512)S(1)} %copy-done.16, f32[512]{0:T(512)S(1)} %add_rsqrt_fusion.1), kind=kOutput, calls=%fused_computation.5 | convolution fusion | flops 4300210176 | bytes 17305600 | tf_op jit(solution)/shard_map/dot_general | solution.py:184
  220.1 4.3 all-to-all-start
  224.5 6.3 %all-to-all-done = bf16[8,2,5120]{2,1,0:T(2,128)(2,1)S(1)} async-done(((bf16[8,2,5120]{2,1,0:T(2,128)(2,1)}), bf16[8,2,5120]{2,1,0:T(2,128)(2,1)S(1)}, u32[]{:S(2)}, u32[]{:S(2)}) %all-to-all-start) | async-done | bytes 163872 | tf_op jit(solution)/shard_map/all_to_all | solution.py:193
  231.3 5.6 %convolution_convert_fusion.3 = bf16[512,8192]{1,0:T(8,128)(2,1)} fusion(bf16[512,80]{1,0:T(8,128)(2,1)S(1)} %reshape.194, bf16[80,8192]{1,0:T(8,128)(2,1)S(1)} %copy-done), kind=kOutput, calls=%fused_computation.4 | convolution fusion | flops 675282944 | bytes 9781248 | tf_op jit(solution)/shard_map/dot_general | solution.py:79
  236.9 11.6 %copy.53 = bf16[64,8,16,512]{3,2,1,0:T(8,128)(2,1)} copy(bf16[64,8,16,512]{3,1,2,0:T(8,128)(2,1)} %bitcast.115) | data formatting | bytes 16777216
  248.4 5.6 %convolution_convert_fusion.2 = bf16[512,8192]{1,0:T(8,128)(2,1)} fusion(bf16[512,80]{1,0:T(8,128)(2,1)S(1)} %reshape.194, bf16[80,8192]{1,0:T(8,128)(2,1)S(1)} %copy-done.3), kind=kOutput, calls=%fused_computation.3 | convolution fusion | flops 675282944 | bytes 9781248 | tf_op jit(solution)/shard_map/dot_general | solution.py:82
  254.0 11.4 %copy.54 = bf16[64,8,16,512]{3,2,1,0:T(8,128)(2,1)} copy(bf16[64,8,16,512]{3,1,2,0:T(8,128)(2,1)} %bitcast.114) | data formatting | bytes 16777216
  265.3 8.4 %pad_maximum_fusion = bf16[16,1024,512]{1,0,2:T(8,128)(2,1)S(1)} fusion(bf16[16,512,512]{1,0,2:T(8,128)(2,1)} %bitcast.117, bf16[16,512,512]{1,0,2:T(8,128)(2,1)} %bitcast.116), kind=kLoop, calls=%fused_computation | loop fusion | flops 33554432 | bytes 33554432 | tf_op jit(solution)/shard_map/concatenate | solution.py:87
  273.7 12.0 %copy.55 = bf16[64,8,16,1024]{3,1,2,0:T(8,128)(2,1)} copy(bf16[64,8,16,1024]{3,2,1,0:T(8,128)(2,1)S(1)} %bitcast.113) | data formatting | bytes 33554432
  286.5 13.1 %reduce-scatter.9.cloned.1.call-done = bf16[512,512]{0,1:T(8,128)(2,1)} async-done(((bf16[8192,512]{0,1:T(8,128)(2,1)}), bf16[512,512]{0,1:T(8,128)(2,1)}) %reduce-scatter.9.cloned.1.call-update) | async-done | bytes 524304 | tf_op jit(solution)/shard_map/reduce_scatter | solution.py:183
  300.8 112.5 %reduce-scatter.7.cloned.1.call-done = bf16[1024,512]{0,1:T(8,128)(2,1)} async-done(((bf16[16384,512]{0,1:T(8,128)(2,1)}), bf16[1024,512]{0,1:T(8,128)(2,1)}) %reduce-scatter.7.cloned.1.call-update) | async-done | bytes 1048592 | tf_op jit(solution)/shard_map/reduce_scatter | solution.py:197
  418.2 6.9 %fusion.1 = bf16[8192,512]{0,1:T(8,128)(2,1)} fusion(bf16[512,512]{1,0:T(8,128)(2,1)S(1)} %bitcast.122, bf16[512,8192]{1,0:T(8,128)(2,1)S(1)} %bitcast.119), kind=kOutput, calls=%fused_computation.6 | convolution fusion | flops 4299161600 | bytes 17301504 | tf_op jit(solution)/shard_map/dot_general | solution.py:223
  426.0 84.6 %reduce-scatter.11.cloned.1.call-done = bf16[512,512]{0,1:T(8,128)(2,1)} async-done(((bf16[8192,512]{0,1:T(8,128)(2,1)}), bf16[512,512]{0,1:T(8,128)(2,1)}) %reduce-scatter.11.cloned.1.call-update) | async-done | bytes 524304 | tf_op jit(solution)/shard_map/reduce_scatter | solution.py:222
  (154 shorter events, 49.3 us)
Async XLA Ops:
  6.5 224.8 %copy-start = (bf16[80,8192]{1,0:T(8,128)(2,1)S(1)}, bf16[80,8192]{1,0:T(8,128)(2,1)}, u32[]{:S(2)}) copy-start(bf16[80,8192]{1,0:T(8,128)(2,1)} %param.35) | copy-start | bytes 3932164
  6.5 78.3 %copy-start.4 = (bf16[4,256,80]{1,2,0:T(8,128)(2,1)S(1)}, bf16[4,256,80]{1,2,0:T(8,128)(2,1)}, u32[]{:S(2)}) copy-start(bf16[4,256,80]{1,2,0:T(8,128)(2,1)} %param.25) | copy-start | bytes 491524
  6.5 160.1 %reduce-scatter.13.cloned.1.call-start = ((), (), s32[]{:S(2)}) async-start(), calls=%async_computation.8 | async-start | bytes 696320
  6.5 10.8 %collective-permute-start = (bf16[4,256,80]{1,2,0:T(8,128)(2,1)}, bf16[4,256,80]{1,2,0:T(8,128)(2,1)S(1)}, u32[]{:S(2)}, u32[]{:S(2)}) collective-permute-start(bf16[4,256,80]{1,2,0:T(8,128)(2,1)} %param.25), channel_id=1, source_target_pairs={{0,1},{1,2},{2,3},{3,4},{4,5},{5,6},{6,7},{7,8},{8,9},{9,10},{10,1... | collective-permute-start | bytes 491528 | tf_op jit(solution)/shard_map/ppermute | solution.py:20
  17.3 8.7 %collective-permute-start.1 = (bf16[4,256,80]{1,2,0:T(8,128)(2,1)S(1)}, bf16[4,256,80]{1,2,0:T(8,128)(2,1)S(1)}, u32[]{:S(2)}, u32[]{:S(2)}) collective-permute-start(bf16[4,256,80]{1,2,0:T(8,128)(2,1)S(1)} %collective-permute-done), channel_id=1, source_target_pairs={{0,1},{1,2},{2,3},{3,4},{4,5},{5,6},{6,7},{7,8},{8,9},{9,10},{10,1... | collective-permute-start | bytes 491528 | tf_op jit(solution)/shard_map/ppermute | solution.py:20
  17.3 8.7 %collective-permute-start.8 = (bf16[4,256,80]{1,2,0:T(8,128)(2,1)}, bf16[4,256,80]{1,2,0:T(8,128)(2,1)S(1)}, u32[]{:S(2)}, u32[]{:S(2)}) collective-permute-start(bf16[4,256,80]{1,2,0:T(8,128)(2,1)} %param.25), channel_id=1, source_target_pairs={{0,15},{1,0},{2,1},{3,2},{4,3},{5,4},{6,5},{7,6},{8,7},{9,8},{10,9... | collective-permute-start | bytes 491528 | tf_op jit(solution)/shard_map/ppermute | solution.py:22
  26.0 8.6 %collective-permute-start.2 = (bf16[4,256,80]{1,2,0:T(8,128)(2,1)S(1)}, bf16[4,256,80]{1,2,0:T(8,128)(2,1)S(1)}, u32[]{:S(2)}, u32[]{:S(2)}) collective-permute-start(bf16[4,256,80]{1,2,0:T(8,128)(2,1)S(1)} %collective-permute-done.1), channel_id=1, source_target_pairs={{0,1},{1,2},{2,3},{3,4},{4,5},{5,6},{6,7},{7,8},{8,9},{9,10},{10,1... | collective-permute-start | bytes 491528 | tf_op jit(solution)/shard_map/ppermute | solution.py:20
  26.0 8.6 %collective-permute-start.9 = (bf16[4,256,80]{1,2,0:T(8,128)(2,1)S(1)}, bf16[4,256,80]{1,2,0:T(8,128)(2,1)S(1)}, u32[]{:S(2)}, u32[]{:S(2)}) collective-permute-start(bf16[4,256,80]{1,2,0:T(8,128)(2,1)S(1)} %collective-permute-done.8), channel_id=1, source_target_pairs={{0,15},{1,0},{2,1},{3,2},{4,3},{5,4},{6,5},{7,6},{8,7},{9,8},{10,9... | collective-permute-start | bytes 491528 | tf_op jit(solution)/shard_map/ppermute | solution.py:22
  34.6 8.6 %collective-permute-start.3 = (bf16[4,256,80]{1,2,0:T(8,128)(2,1)S(1)}, bf16[4,256,80]{1,2,0:T(8,128)(2,1)S(1)}, u32[]{:S(2)}, u32[]{:S(2)}) collective-permute-start(bf16[4,256,80]{1,2,0:T(8,128)(2,1)S(1)} %collective-permute-done.2), channel_id=1, source_target_pairs={{0,1},{1,2},{2,3},{3,4},{4,5},{5,6},{6,7},{7,8},{8,9},{9,10},{10,1... | collective-permute-start | bytes 491528 | tf_op jit(solution)/shard_map/ppermute | solution.py:20
  34.7 9.7 %collective-permute-start.10 = (bf16[4,256,80]{1,2,0:T(8,128)(2,1)S(1)}, bf16[4,256,80]{1,2,0:T(8,128)(2,1)S(1)}, u32[]{:S(2)}, u32[]{:S(2)}) collective-permute-start(bf16[4,256,80]{1,2,0:T(8,128)(2,1)S(1)} %collective-permute-done.9), channel_id=1, source_target_pairs={{0,15},{1,0},{2,1},{3,2},{4,3},{5,4},{6,5},{7,6},{8,7},{9,8},{10,9... | collective-permute-start | bytes 491528 | tf_op jit(solution)/shard_map/ppermute | solution.py:22
  43.3 8.6 %collective-permute-start.4 = (bf16[4,256,80]{1,2,0:T(8,128)(2,1)S(1)}, bf16[4,256,80]{1,2,0:T(8,128)(2,1)S(1)}, u32[]{:S(2)}, u32[]{:S(2)}) collective-permute-start(bf16[4,256,80]{1,2,0:T(8,128)(2,1)S(1)} %collective-permute-done.3), channel_id=1, source_target_pairs={{0,1},{1,2},{2,3},{3,4},{4,5},{5,6},{6,7},{7,8},{8,9},{9,10},{10,1... | collective-permute-start | bytes 491528 | tf_op jit(solution)/shard_map/ppermute | solution.py:20
  44.4 8.2 %collective-permute-start.11 = (bf16[4,256,80]{1,2,0:T(8,128)(2,1)S(1)}, bf16[4,256,80]{1,2,0:T(8,128)(2,1)S(1)}, u32[]{:S(2)}, u32[]{:S(2)}) collective-permute-start(bf16[4,256,80]{1,2,0:T(8,128)(2,1)S(1)} %collective-permute-done.10), channel_id=1, source_target_pairs={{0,15},{1,0},{2,1},{3,2},{4,3},{5,4},{6,5},{7,6},{8,7},{9,8},{10,9... | collective-permute-start | bytes 491528 | tf_op jit(solution)/shard_map/ppermute | solution.py:22
  51.9 8.9 %collective-permute-start.5 = (bf16[4,256,80]{1,2,0:T(8,128)(2,1)S(1)}, bf16[4,256,80]{1,2,0:T(8,128)(2,1)S(1)}, u32[]{:S(2)}, u32[]{:S(2)}) collective-permute-start(bf16[4,256,80]{1,2,0:T(8,128)(2,1)S(1)} %collective-permute-done.4), channel_id=1, source_target_pairs={{0,1},{1,2},{2,3},{3,4},{4,5},{5,6},{6,7},{7,8},{8,9},{9,10},{10,1... | collective-permute-start | bytes 491528 | tf_op jit(solution)/shard_map/ppermute | solution.py:20
  52.6 9.7 %collective-permute-start.12 = (bf16[4,256,80]{1,2,0:T(8,128)(2,1)S(1)}, bf16[4,256,80]{1,2,0:T(8,128)(2,1)S(1)}, u32[]{:S(2)}, u32[]{:S(2)}) collective-permute-start(bf16[4,256,80]{1,2,0:T(8,128)(2,1)S(1)} %collective-permute-done.11), channel_id=1, source_target_pairs={{0,15},{1,0},{2,1},{3,2},{4,3},{5,4},{6,5},{7,6},{8,7},{9,8},{10,9... | collective-permute-start | bytes 491528 | tf_op jit(solution)/shard_map/ppermute | solution.py:22
  60.8 9.9 %collective-permute-start.6 = (bf16[4,256,80]{1,2,0:T(8,128)(2,1)S(1)}, bf16[4,256,80]{1,2,0:T(8,128)(2,1)}, u32[]{:S(2)}, u32[]{:S(2)}) collective-permute-start(bf16[4,256,80]{1,2,0:T(8,128)(2,1)S(1)} %collective-permute-done.5), channel_id=1, source_target_pairs={{0,1},{1,2},{2,3},{3,4},{4,5},{5,6},{6,7},{7,8},{8,9},{9,10},{10,1... | collective-permute-start | bytes 491528 | tf_op jit(solution)/shard_map/ppermute | solution.py:20
  62.3 9.9 %collective-permute-start.13 = (bf16[4,256,80]{1,2,0:T(8,128)(2,1)S(1)}, bf16[4,256,80]{1,2,0:T(8,128)(2,1)S(1)}, u32[]{:S(2)}, u32[]{:S(2)}) collective-permute-start(bf16[4,256,80]{1,2,0:T(8,128)(2,1)S(1)} %collective-permute-done.12), channel_id=1, source_target_pairs={{0,15},{1,0},{2,1},{3,2},{4,3},{5,4},{6,5},{7,6},{8,7},{9,8},{10,9... | collective-permute-start | bytes 491528 | tf_op jit(solution)/shard_map/ppermute | solution.py:22
  70.7 9.0 %collective-permute-start.7 = (bf16[4,256,80]{1,2,0:T(8,128)(2,1)}, bf16[4,256,80]{1,2,0:T(8,128)(2,1)}, u32[]{:S(2)}, u32[]{:S(2)}) collective-permute-start(bf16[4,256,80]{1,2,0:T(8,128)(2,1)} %collective-permute-done.6), channel_id=1, source_target_pairs={{0,1},{1,2},{2,3},{3,4},{4,5},{5,6},{6,7},{7,8},{8,9},{9,10},{10,1... | collective-permute-start | bytes 491528 | tf_op jit(solution)/shard_map/ppermute | solution.py:20
  72.1 10.6 %collective-permute-start.14 = (bf16[4,256,80]{1,2,0:T(8,128)(2,1)S(1)}, bf16[4,256,80]{1,2,0:T(8,128)(2,1)S(1)}, u32[]{:S(2)}, u32[]{:S(2)}) collective-permute-start(bf16[4,256,80]{1,2,0:T(8,128)(2,1)S(1)} %collective-permute-done.13), channel_id=1, source_target_pairs={{0,15},{1,0},{2,1},{3,2},{4,3},{5,4},{6,5},{7,6},{8,7},{9,8},{10,9... | collective-permute-start | bytes 491528 | tf_op jit(solution)/shard_map/ppermute | solution.py:22
  87.6 119.3 %copy-start.16 = (f32[512]{0:T(512)S(1)}, f32[512]{0:T(512)}, u32[]{:S(2)}) copy-start(f32[512]{0:T(512)} %param.20) | copy-start | bytes 6148
  93.1 206.5 %reduce-scatter.9.cloned.1.call-start = ((), (), s32[]{:S(2)}) async-start(), calls=%async_computation.6 | async-start | bytes 8912896 | tf_op jit(solution)/shard_map/reduce_scatter | solution.py:183
  220.1 10.8 %all-to-all-start = ((bf16[8,2,5120]{2,1,0:T(2,128)(2,1)}), bf16[8,2,5120]{2,1,0:T(2,128)(2,1)S(1)}, u32[]{:S(2)}, u32[]{:S(2)}) async-start(bf16[8,2,5120]{2,1,0:T(2,128)(2,1)} %copy.39), calls=%async_computation | async-start | bytes 327680 | tf_op jit(solution)/shard_map/all_to_all | solution.py:193
  224.4 188.9 %reduce-scatter.7.cloned.1.call-start = ((), (), s32[]{:S(2)}) async-start(), calls=%async_computation.5 | async-start | bytes 17825792 | tf_op jit(solution)/shard_map/reduce_scatter | solution.py:197
  285.8 224.8 %reduce-scatter.11.cloned.1.call-start = ((), (), s32[]{:S(2)}) async-start(), calls=%async_computation.7 | async-start | bytes 8912896 | tf_op jit(solution)/shard_map/reduce_scatter | solution.py:222
  425.2 87.6 %copy-start.1 = (bf16[80,8192]{1,0:T(8,128)(2,1)S(1)}, bf16[80,8192]{1,0:T(8,128)(2,1)}, u32[]{:S(2)}) copy-start(bf16[80,8192]{1,0:T(8,128)(2,1)} %param.35) | copy-start | bytes 3932164
  (15 other events, 51.6 us)
Sparse Core Ops, SparseCore 0:
  93.2 73.3 reduce-scatter.12
  217.2 82.2 reduce-scatter.8
  302.9 110.2 reduce-scatter.6
  425.3 85.1 reduce-scatter.10
